TPU v7x, 256 devices: a whole 4x4x8 slice. The times are simulated.
256 devices in a mesh: row: 4 (over y), col: 4 (over x), dp: 16 (over z, core).
Axes of the slice: x: 4, y: 4, z: 8, core: 2. Of those that a mesh axis runs over, the one named last changes fastest.
Arguments:
- hidden_states: bfloat16 [16384, 1536], P(('dp', 'row'), 'col'), may hold values from -18 to 18
- w_query: bfloat16 [1536, 1536], P('col', 'row'), may hold values from -0.102062073 to 0.102062073
- w_key_value: bfloat16 [1536, 512], P('col'), may hold values from -0.102062073 to 0.102062073
- adapter_down: bfloat16 [1024, 1536, 16], P('dp', 'col'), may hold values from -0.15625 to 0.15625
- adapter_up: bfloat16 [1024, 16, 1536], P('dp', None, 'row'), may hold values from -1.5 to 1.5
- req_lengths: int32 [16, 8], replicated, may hold values from 1 to 160, 960 in all within a row
- req_adapter: int32 [16, 8], replicated, may hold values from 0 to 1023, as said below
Outputs:
- attention: bfloat16 [16384, 1536], P(('dp', 'col'), 'row')
- kv_cache: bfloat16 [16384, 512], P(('dp', 'col'))
Inputs may be any that keep to these rules, and one draw needn't show every extreme that they name: `req_lengths`: the lengths of one block sum to 960, and each block has a request of exactly 160 tokens. `req_adapter`: adapters k * 64 to (k + 1) * 64 - 1 are those of index k of dp; the requests of one block use adapters of one index of dp at most 1 times, and some index of dp is used exactly that often by every block.
All inputs are finite; a program needn't handle non-finite values.
Results may differ from a plain program's by a relative error of at most 0.0072.
Values may be sent and summed in bfloat16 or wider, within the bound.
No kernel may reach another device: no remote copies, remote signals or barrier semaphores. Data moves between devices by JAX's collectives and lax.ppermute only.
A program may use at most 128 MiB of HBM per device.

v0:
```python
import math
import jax
import jax.numpy as jnp
from jax import lax
from jax.sharding import PartitionSpec as P

HEAD_DIM = 128
MOST_LEN = 160
masked_score = -1e30


def block_layout(lengths_row, block_len):
    prefix_len = block_len - jnp.sum(lengths_row)
    ends_at = jnp.cumsum(lengths_row) + prefix_len
    starts = ends_at - lengths_row
    positions = jnp.arange(block_len, dtype=jnp.int32)
    segment = jnp.sum((positions[:, None] >= starts[None, :]).astype(jnp.int32), axis=1)
    return (starts, segment, positions)


def slot_numbers(holders):
    request_total = holders.shape[0]
    ordering = jnp.arange(request_total, dtype=jnp.int32)
    earlier = ordering[None, :] < ordering[:, None]
    same_holder = holders[:, None] == holders[None, :]
    return jnp.sum((earlier & same_holder).astype(jnp.int32), axis=1)


def make_attend(query_rows, segment, first_row, kv_group, head_size, kv_half):
    own_rows = query_rows.shape[0]
    heads_here = query_rows.shape[1] // head_size
    query_heads = query_rows.reshape(own_rows, heads_here, head_size)
    query_pos = first_row + jnp.arange(own_rows, dtype=jnp.int32)
    query_seg = lax.dynamic_slice_in_dim(segment, first_row, own_rows, 0)
    score_scale = 1.0 / math.sqrt(head_size)

    def attend(state_in, key_block, key_start):
        running_max, running_sum, running_out = state_in
        block_size = key_block.shape[0]
        key_rows = lax.dynamic_slice_in_dim(key_block, kv_group * head_size, head_size, 1)
        values = lax.dynamic_slice_in_dim(key_block, kv_half + kv_group * head_size, head_size, 1)
        key_pos = jnp.arange(block_size, dtype=jnp.int32)
        allowed = (key_pos[None, :] <= query_pos[:, None]) & (
            (segment[None, :] == query_seg[:, None]) | (segment[None, :] == 0)
        )
        scores = (
            jnp.einsum("qhd,kd->hqk", query_heads, key_rows, preferred_element_type=jnp.float32)
            * score_scale
        )
        scores = jnp.where(allowed[None], scores, masked_score)
        new_max = jnp.maximum(running_max, jnp.max(scores, axis=2))
        weights = jnp.where(allowed[None], jnp.exp(scores - new_max[:, :, None]), 0.0)
        running_sum = jnp.sum(weights, axis=2)
        running_out = jnp.einsum(
            "hqk,kd->hqd", weights.astype(jnp.bfloat16), values, preferred_element_type=jnp.float32
        )
        return (new_max, running_sum, running_out)

    initial = (
        jnp.full((heads_here, own_rows), masked_score, jnp.float32),
        jnp.zeros((heads_here, own_rows), jnp.float32),
        jnp.zeros((heads_here, own_rows, head_size), jnp.float32),
    )
    return (attend, initial)


def body(hidden_states, w_query, w_key_value, adapter_down, adapter_up, req_lengths, req_adapter):
    dp_size = lax.axis_size("dp")
    block_index = lax.axis_index("dp")
    col_index = lax.axis_index("col")
    row_index = lax.axis_index("row")
    gathered = lax.all_gather(hidden_states, "row", axis=0, tiled=True)
    block_len = gathered.shape[0]
    query_cols = w_query.shape[1]
    kv_cols = w_key_value.shape[1]
    kv_half = kv_cols // 2
    head_size = HEAD_DIM
    heads_here = query_cols // head_size
    heads_total = heads_here * lax.axis_size("row")
    kv_heads = kv_half // head_size
    kv_group = row_index * heads_here // (heads_total // kv_heads)
    own_rows = block_len // lax.axis_size("col")
    first_row = col_index * own_rows
    held_sets = adapter_down.shape[0]
    width_here = adapter_down.shape[1]
    rank_size = adapter_down.shape[2]
    lengths_row = req_lengths[block_index]
    adapters_row = req_adapter[block_index]
    requests = lengths_row.shape[0]
    starts, segment, positions = block_layout(lengths_row, block_len)
    request_of = jnp.clip(segment - 1, 0, requests - 1)
    in_request = segment > 0
    holders = adapters_row // held_sets
    wanted_from_me = req_adapter // held_sets == block_index
    local_pick = jnp.sum(jnp.where(wanted_from_me, req_adapter % held_sets, 0), axis=1)
    down_pick = jnp.transpose(jnp.take(adapter_down, local_pick, axis=0), (0, 2, 1))
    up_pick = jnp.take(adapter_up, local_pick, axis=0)
    outgoing = jnp.concatenate([down_pick, up_pick], axis=1)
    incoming = lax.all_to_all(outgoing, "dp", split_axis=0, concat_axis=0, tiled=True)
    flat_down = incoming[:, :rank_size, :].reshape(dp_size * rank_size, width_here).T
    flat_up = (
        incoming[:, rank_size:, :].reshape(dp_size * rank_size, query_cols).astype(jnp.float32)
    )
    rank_owner = jnp.arange(dp_size * rank_size, dtype=jnp.int32) // rank_size
    reduced = jnp.dot(gathered, flat_down, preferred_element_type=jnp.float32)
    request_ids = jnp.arange(requests, dtype=jnp.int32)
    token_holder = (
        jnp.sum(
            jnp.where(segment[:, None] == request_ids[None, :] + 1, holders[None, :] + 1, 0), axis=1
        )
        - 1
    )
    kept_cols = rank_owner[None, :] == token_holder[:, None]
    reduced = jnp.where(kept_cols, reduced, 0.0)
    adapter_term = jnp.dot(reduced, flat_up, precision=lax.Precision.HIGHEST)
    kv_share = kv_cols // lax.axis_size("row")
    kv_slice = lax.dynamic_slice_in_dim(w_key_value, row_index * kv_share, kv_share, 1)
    both_weights = jnp.concatenate([w_query, kv_slice], axis=1)
    partial_value = jnp.dot(gathered, both_weights, preferred_element_type=jnp.float32)
    summed = lax.psum_scatter(
        partial_value
        + jnp.concatenate(
            [adapter_term, jnp.zeros((own_rows * lax.axis_size("col"), kv_share), jnp.float32)],
            axis=1,
        ),
        "col",
        scatter_dimension=0,
        tiled=True,
    )
    query_rows = summed[:, :query_cols].astype(jnp.bfloat16)
    kv_pieces = lax.all_gather(summed[:, query_cols:].astype(jnp.bfloat16), ("row", "col"), axis=0)
    kv_pieces = kv_pieces.reshape(lax.axis_size("row"), lax.axis_size("col"), own_rows, kv_share)
    own_pieces = lax.dynamic_index_in_dim(kv_pieces, col_index, 1, keepdims=False)
    kv_cache = jnp.transpose(own_pieces, (1, 0, 2)).reshape(own_rows, kv_cols)
    parts_per_head = head_size // kv_share
    key_all = lax.dynamic_slice_in_dim(kv_pieces, kv_group * parts_per_head, parts_per_head, 0)
    value_all = lax.dynamic_slice_in_dim(
        kv_pieces, (kv_heads + kv_group) * parts_per_head, parts_per_head, 0
    )
    key_all = jnp.transpose(key_all, (1, 2, 0, 3)).reshape(block_len, head_size)
    value_all = jnp.transpose(value_all, (1, 2, 0, 3)).reshape(block_len, head_size)
    attend, initial = make_attend(query_rows, segment, first_row, 0, head_size, head_size)
    running_max, running_sum, running_out = attend(
        initial, jnp.concatenate([key_all, value_all], axis=1), jnp.int32(0)
    )
    attention = (running_out / running_sum[:, :, None]).astype(jnp.bfloat16)
    attention = jnp.transpose(attention, (1, 0, 2)).reshape(own_rows, query_cols)
    return (attention, kv_cache)


def solution(mesh):
    return jax.shard_map(
        body,
        mesh=mesh,
        in_specs=(
            P(("dp", "row"), "col"),
            P("col", "row"),
            P("col", None),
            P("dp", "col", None),
            P("dp", None, "row"),
            P(),
            P(),
        ),
        out_specs=(P(("dp", "col"), "row"), P(("dp", "col"), None)),
        check_vma=False,
    )
```

profile of v0, /device:TPU:2, one launch (start us, length us, event | category | flops | bytes accessed | tf_op | source)
XLA Modules:
  0.0 139.3 jit_solution(9572171960682573029)
XLA Ops:
  7.2 0.0 copy-start
  7.2 0.0 copy-start.3
  7.2 0.0 copy-start.4
  7.2 0.0 copy-start.2
  7.2 0.8 fusion.25
  8.0 0.3 copy-done
  8.3 0.6 gather_fusion.1
  8.9 1.7 %gather_fusion = bf16[16,384,16]{1,2,0:T(8,128)(2,1)S(1)} fusion(bf16[64,384,16]{1,2,0:T(8,128)(2,1)} %param.10, s32[1024]{0:T(1024)S(1)} %pad_clamp_fusion), kind=kCustom, calls=%fused_computation | custom fusion | bytes 393280 | tf_op jit(solution)/shard_map/jit(_take)/gather | solution.py:96
  10.6 0.1 broadcast_select_fusion
  10.7 0.1 select_bitcast_fusion
  10.9 0.8 pad_maximum_fusion
  11.6 8.6 %all-to-all-start = ((bf16[16,32,384]{2,1,0:T(8,128)(2,1)}), bf16[16,32,384]{2,1,0:T(8,128)(2,1)S(1)}, u32[]{:S(2)}, u32[]{:S(2)}) async-start(bf16[16,32,384]{2,1,0:T(8,128)(2,1)} %pad_maximum_fusion), calls=%async_computation | async-start | bytes 786432 | tf_op jit(solution)/shard_map/all_to_all | solution.py:99
  20.2 0.0 reduce-scatter.2.cloned.1.call-start
  20.3 0.0 copy-done.3
  20.3 0.0 copy-done.4
  20.3 0.7 fusion.34
  21.7 0.1 subtract_reduce_fusion
  21.8 0.1 convert_reduce_fusion
  21.9 0.9 constant_dynamic-slice_fusion.3
  22.8 0.1 select_reduce_fusion
  22.9 0.0 copy-done.2
  22.9 0.0 copy-start.1
  22.9 14.5 %all_gather.9 = bf16[1024,384]{1,0:T(8,128)(2,1)S(1)} all-gather(bf16[256,384]{1,0:T(8,128)(2,1)S(1)} %copy-done.2), channel_id=1, replica_groups=mesh['row'=4,'col'=4,'dp'=16] {'row'}, dimensions={0}, use_global_device_ids=true | all-gather | bytes 983040 | tf_op jit(solution)/shard_map/all_gather | solution.py:72
  37.4 0.0 all-to-all-done
  37.4 0.5 fusion.6
  37.9 0.9 fusion.36
  38.8 0.0 copy-done.1
  38.8 2.1 %bitcast_add_fusion = f32[1024,512]{0,1:T(8,128)} fusion(f32[1024,384]{0,1:T(8,128)S(1)} %fusion.36, bf16[1024,384]{1,0:T(8,128)(2,1)S(1)} %all_gather.9, bf16[384,128]{1,0:T(8,128)(2,1)S(1)} %constant_dynamic-slice_fusion.3, bf16[384,384]{1,0:T(8,128)(2,1)S(1)} %copy-done.1), kind=kOutput, calls=%fused_computation.7 | convolution fusion | flops 403963904 | bytes 4849664 | tf_op jit(solution)/shard_map/dot_general | solution.py:119
  40.9 0.0 reduce-scatter.2.cloned.1.call-update
  41.0 0.0 all-gather.3.cloned.1.call-start
  41.0 32.3 %reduce-scatter.2.cloned.1.call-done = f32[256,512]{0,1:T(8,128)} async-done(((f32[1024,512]{0,1:T(8,128)}), f32[256,512]{0,1:T(8,128)}) %reduce-scatter.2.cloned.1.call-update) | async-done | bytes 524304 | tf_op jit(solution)/shard_map/reduce_scatter | solution.py:120
  73.3 1.1 convert.4
  74.4 0.6 slice.24
  75.0 0.0 all-gather.3.cloned.1.call-update
  75.1 0.1 dynamic_slice.23
  75.2 0.8 fusion.10
  76.0 49.1 %all-gather.3.cloned.1.call-done = bf16[4096,128]{0,1:T(8,128)(2,1)} async-done(((bf16[256,128]{0,1:T(8,128)(2,1)}), bf16[4096,128]{0,1:T(8,128)(2,1)}) %all-gather.3.cloned.1.call-update) | async-done | bytes 1048592 | tf_op jit(solution)/shard_map/all_gather | solution.py:131
  125.1 1.8 %reshape.151 = bf16[4,4,256,128]{2,1,0,3:T(4,128)(2,1)S(1)} reshape(bf16[4096,128]{0,1:T(8,128)(2,1)} %all-gather.3.cloned.1.call-done) | data formatting | bytes 2097152 | tf_op jit(solution)/shard_map/reshape | solution.py:132
  127.0 0.5 constant_dynamic-slice_fusion.2
  127.6 0.1 copy.40
  127.6 0.8 copy.35
  128.5 0.2 constant_dynamic-slice_fusion.1
  128.7 0.2 copy.29
  128.9 0.2 reshape.174
  129.1 0.7 fusion
  129.8 0.8 fusion.1
  130.6 1.0 fusion.14
  131.6 0.8 copy.34
  (12 shorter events, 0.1 us)
Async XLA Ops:
  7.2 1.2 copy-start
  7.2 13.1 %copy-start.3 = (s32[16,8]{0,1:T(8,128)S(1)}, s32[16,8]{0,1:T(8,128)}, u32[]{:S(2)}) copy-start(s32[16,8]{0,1:T(8,128)} %param.13) | copy-start | bytes 1540
  7.2 13.1 %copy-start.4 = (s32[16,8]{0,1:T(8,128)S(1)}, s32[16,8]{0,1:T(8,128)}, u32[]{:S(2)}) copy-start(s32[16,8]{0,1:T(8,128)} %param.12) | copy-start | bytes 1540
  7.2 15.7 %copy-start.2 = (bf16[256,384]{1,0:T(8,128)(2,1)S(1)}, bf16[256,384]{1,0:T(8,128)(2,1)}, u32[]{:S(2)}) copy-start(bf16[256,384]{1,0:T(8,128)(2,1)} %param.7) | copy-start | bytes 589828
  11.6 25.8 %all-to-all-start = ((bf16[16,32,384]{2,1,0:T(8,128)(2,1)}), bf16[16,32,384]{2,1,0:T(8,128)(2,1)S(1)}, u32[]{:S(2)}, u32[]{:S(2)}) async-start(bf16[16,32,384]{2,1,0:T(8,128)(2,1)} %pad_maximum_fusion), calls=%async_computation | async-start | bytes 786432 | tf_op jit(solution)/shard_map/all_to_all | solution.py:99
  20.2 53.1 %reduce-scatter.2.cloned.1.call-start = ((), (), s32[]{:S(2)}) async-start(), calls=%async_computation.2 | async-start | bytes 2621440 | tf_op jit(solution)/shard_map/reduce_scatter | solution.py:120
  22.9 15.9 %copy-start.1 = (bf16[384,384]{1,0:T(8,128)(2,1)S(1)}, bf16[384,384]{1,0:T(8,128)(2,1)}, u32[]{:S(2)}) copy-start(bf16[384,384]{1,0:T(8,128)(2,1)} %param.8) | copy-start | bytes 884740
  41.0 84.2 %all-gather.3.cloned.1.call-start = ((), (), s32[]{:S(2)}) async-start(), calls=%async_computation.3 | async-start | bytes 1114112 | tf_op jit(solution)/shard_map/all_gather | solution.py:131
Sparse Core Ops, SparseCore 0:
  41.1 32.1 reduce-scatter.1
  76.3 48.8 all-gather.2
where the time goes:
time: 140 us; the launch traced here: 139 us
  waiting for transfers between devices  81.5 us (58%)
  between operations  15 us (11%)
  blocking collectives  14.5 us (10%)
  local copies, waits for them, and re-layouts  9.02 us (6%)
  starting transfers between devices  8.65 us (6%)
  other arithmetic  5.54 us (4%)
  matrix products  5.16 us (4%)
    all_gather x1, waiting for transfers between devices, body(): lax.all_gather(summed[:, query_cols:].astype(jnp.bfloat16), ('row', 'col'...  49.1 us
    reduce_scatter x1, waiting for transfers between devices, body(): lax.psum_scatter(partial_value + jnp.concatenate([adapter_term, jnp.zeros...  32.3 us
    all_gather x1, blocking collectives, body(): gathered = lax.all_gather(hidden_states, 'row', axis=0, tiled=True)  14.5 us
    all_to_all x1, starting transfers between devices, body(): lax.all_to_all(outgoing, 'dp', split_axis=0, concat_axis=0, tiled=True)  8.57 us
  transfers between devices with their start and end apart: 3, of which 2 were waited for; matrix products, arithmetic and copies ran while one was open for 2% of the time, Pallas kernels for 0%

commit v1 on v0

--- a/solution.py
+++ b/solution.py
@@ -69,7 +69,9 @@
     block_index = lax.axis_index("dp")
     col_index = lax.axis_index("col")
     row_index = lax.axis_index("row")
-    gathered = lax.all_gather(hidden_states, "row", axis=0, tiled=True)
+    gathered = jnp.concatenate(
+        lax.all_to_all(jnp.stack([hidden_states] * lax.axis_size("row")), "row", 0, 0), axis=0
+    )
     block_len = gathered.shape[0]
     query_cols = w_query.shape[1]
     kv_cols = w_key_value.shape[1]

time: 140 us -> 149 us (1.064)
  waiting for transfers between devices: 81.5 us -> 99.8 us
  blocking collectives: 14.5 us -> 0 us
  starting transfers between devices: 8.65 us -> 13.1 us
    all_gather x1 -> x0, blocking collectives: 14.5 us -> none  [body(): gathered = lax.all_gather(hidden_states, 'row', axis=0, tiled=True)]
    all_to_all x0 -> x1, waiting for transfers between devices: none -> 13.5 us  [body(): lax.all_to_all(jnp.stack([hidden_states] * lax.axis_size('row')), 'row',...]
    all_to_all x1, waiting for transfers between devices: 0.01 us -> 11.1 us  [body(): lax.all_to_all(outgoing, 'dp', split_axis=0, concat_axis=0, tiled=True)]
    reduce_scatter x1, waiting for transfers between devices: 32.3 us -> 26.1 us  [body(): lax.psum_scatter(partial_value + jnp.concatenate([adapter_term, jnp.zeros...]
    all_to_all x0 -> x1, starting transfers between devices: none -> 4.46 us  [body(): lax.all_to_all(jnp.stack([hidden_states] * lax.axis_size('row')), 'row',...]
  transfers between devices with their start and end apart: 3 -> 4, of which waited for: 2 -> 4; matrix products, arithmetic and copies ran while one was open for 2% -> 2% of each run, Pallas kernels for 0% -> 0%
where the time goes in v1:
time: 149 us
  waiting for transfers between devices  99.8 us (67%)
  between operations  15 us (10%)
  starting transfers between devices  13.1 us (9%)
  local copies, waits for them, and re-layouts  9.96 us (7%)
  other arithmetic  5.54 us (4%)
  matrix products  5.16 us (3%)
    all_gather x1, waiting for transfers between devices, body(): lax.all_gather(summed[:, query_cols:].astype(jnp.bfloat16), ('row', 'col'...  49.2 us
    reduce_scatter x1, waiting for transfers between devices, body(): lax.psum_scatter(partial_value + jnp.concatenate([adapter_term, jnp.zeros...  26.1 us
    all_to_all x1, waiting for transfers between devices, body(): lax.all_to_all(jnp.stack([hidden_states] * lax.axis_size('row')), 'row',...  13.5 us
    all_to_all x1, waiting for transfers between devices, body(): lax.all_to_all(outgoing, 'dp', split_axis=0, concat_axis=0, tiled=True)  11.1 us
    all_to_all x1, starting transfers between devices, body(): lax.all_to_all(outgoing, 'dp', split_axis=0, concat_axis=0, tiled=True)  8.57 us
    all_to_all x1, starting transfers between devices, body(): lax.all_to_all(jnp.stack([hidden_states] * lax.axis_size('row')), 'row',...  4.46 us
  transfers between devices with their start and end apart: 4, of which 4 were waited for; matrix products, arithmetic and copies ran while one was open for 2% of the time, Pallas kernels for 0%

profile of v1, /device:TPU:2, one launch (start us, length us, event | category | flops | bytes accessed | tf_op | source)
XLA Modules:
  0.0 148.5 jit_solution(4222879028124026218)
XLA Ops:
  7.2 0.0 copy-start
  7.2 0.0 copy-start.3
  7.2 0.0 copy-start.4
  7.2 0.0 copy-start.2
  7.2 0.8 fusion.25
  8.0 0.3 copy-done
  8.3 0.6 gather_fusion.1
  8.9 1.7 %gather_fusion = bf16[16,384,16]{1,2,0:T(8,128)(2,1)S(1)} fusion(bf16[64,384,16]{1,2,0:T(8,128)(2,1)} %param.10, s32[1024]{0:T(1024)S(1)} %pad_clamp_fusion), kind=kCustom, calls=%fused_computation | custom fusion | bytes 393280 | tf_op jit(solution)/shard_map/jit(_take)/gather | solution.py:98
  10.6 0.1 broadcast_select_fusion
  10.7 0.1 select_bitcast_fusion
  10.9 0.8 pad_maximum_fusion
  11.6 8.6 %all-to-all-start.1 = ((bf16[16,32,384]{2,1,0:T(8,128)(2,1)}), bf16[16,32,384]{2,1,0:T(8,128)(2,1)S(1)}, u32[]{:S(2)}, u32[]{:S(2)}) async-start(bf16[16,32,384]{2,1,0:T(8,128)(2,1)} %pad_maximum_fusion), calls=%async_computation.1 | async-start | bytes 786432 | tf_op jit(solution)/shard_map/all_to_all | solution.py:101
  20.2 0.0 copy-done.3
  20.2 0.0 copy-done.4
  20.2 0.7 fusion.34
  21.7 0.1 subtract_reduce_fusion
  21.8 0.1 convert_reduce_fusion
  21.9 0.9 constant_dynamic-slice_fusion.3
  22.8 11.1 %all-to-all-done.1 = bf16[16,32,384]{2,1,0:T(8,128)(2,1)S(1)} async-done(((bf16[16,32,384]{2,1,0:T(8,128)(2,1)}), bf16[16,32,384]{2,1,0:T(8,128)(2,1)S(1)}, u32[]{:S(2)}, u32[]{:S(2)}) %all-to-all-start.1) | async-done | bytes 393248 | tf_op jit(solution)/shard_map/all_to_all | solution.py:101
  33.8 0.0 copy-done.2
  33.8 0.9 stack.2
  34.8 4.5 %all-to-all-start = ((bf16[4,256,384]{2,1,0:T(8,128)(2,1)}), bf16[4,256,384]{2,1,0:T(8,128)(2,1)S(1)}, u32[]{:S(2)}, u32[]{:S(2)}) async-start(bf16[4,256,384]{2,1,0:T(8,128)(2,1)} %stack.2), calls=%async_computation | async-start | bytes 1572864 | tf_op jit(solution)/shard_map/all_to_all | solution.py:73
  39.3 0.0 copy-start.1
  39.3 0.0 reduce-scatter.2.cloned.1.call-start
  39.3 0.1 select_reduce_fusion
  39.4 13.5 %all-to-all-done = bf16[4,256,384]{2,1,0:T(8,128)(2,1)S(1)} async-done(((bf16[4,256,384]{2,1,0:T(8,128)(2,1)}), bf16[4,256,384]{2,1,0:T(8,128)(2,1)S(1)}, u32[]{:S(2)}, u32[]{:S(2)}) %all-to-all-start) | async-done | bytes 786464 | tf_op jit(solution)/shard_map/all_to_all | solution.py:73
  52.9 0.5 fusion.6
  53.4 0.9 fusion.36
  54.3 0.0 copy-done.1
  54.3 2.1 %bitcast_add_fusion = f32[1024,512]{0,1:T(8,128)} fusion(f32[1024,384]{0,1:T(8,128)S(1)} %fusion.36, bf16[1024,384]{1,0:T(8,128)(2,1)S(1)} %bitcast.63, bf16[384,128]{1,0:T(8,128)(2,1)S(1)} %constant_dynamic-slice_fusion.3, bf16[384,384]{1,0:T(8,128)(2,1)S(1)} %copy-done.1), kind=kOutput, calls=%fused_computation.7 | convolution fusion | flops 403963904 | bytes 4849664 | tf_op jit(solution)/shard_map/dot_general | solution.py:121
  56.4 0.0 reduce-scatter.2.cloned.1.call-update
  56.5 0.0 all-gather.3.cloned.1.call-start
  56.5 26.1 %reduce-scatter.2.cloned.1.call-done = f32[256,512]{0,1:T(8,128)} async-done(((f32[1024,512]{0,1:T(8,128)}), f32[256,512]{0,1:T(8,128)}) %reduce-scatter.2.cloned.1.call-update) | async-done | bytes 524304 | tf_op jit(solution)/shard_map/reduce_scatter | solution.py:122
  82.6 1.1 convert.4
  83.6 0.6 slice.24
  84.3 0.0 all-gather.3.cloned.1.call-update
  84.3 0.1 dynamic_slice.23
  84.4 0.8 fusion.10
  85.3 49.2 %all-gather.3.cloned.1.call-done = bf16[4096,128]{0,1:T(8,128)(2,1)} async-done(((bf16[256,128]{0,1:T(8,128)(2,1)}), bf16[4096,128]{0,1:T(8,128)(2,1)}) %all-gather.3.cloned.1.call-update) | async-done | bytes 1048592 | tf_op jit(solution)/shard_map/all_gather | solution.py:133
  134.4 1.8 %reshape.157 = bf16[4,4,256,128]{2,1,0,3:T(4,128)(2,1)S(1)} reshape(bf16[4096,128]{0,1:T(8,128)(2,1)} %all-gather.3.cloned.1.call-done) | data formatting | bytes 2097152 | tf_op jit(solution)/shard_map/reshape | solution.py:134
  136.3 0.5 constant_dynamic-slice_fusion.2
  136.8 0.1 copy.40
  136.9 0.8 copy.35
  137.8 0.2 constant_dynamic-slice_fusion.1
  137.9 0.2 copy.29
  138.2 0.2 reshape.180
  138.4 0.7 fusion
  139.1 0.8 fusion.1
  139.9 1.0 fusion.14
  140.9 0.8 copy.34
  (12 shorter events, 0.1 us)
Async XLA Ops:
  7.2 1.2 copy-start
  7.2 13.0 %copy-start.3 = (s32[16,8]{0,1:T(8,128)S(1)}, s32[16,8]{0,1:T(8,128)}, u32[]{:S(2)}) copy-start(s32[16,8]{0,1:T(8,128)} %param.13) | copy-start | bytes 1540
  7.2 13.0 %copy-start.4 = (s32[16,8]{0,1:T(8,128)S(1)}, s32[16,8]{0,1:T(8,128)}, u32[]{:S(2)}) copy-start(s32[16,8]{0,1:T(8,128)} %param.12) | copy-start | bytes 1540
  7.2 26.6 %copy-start.2 = (bf16[256,384]{1,0:T(8,128)(2,1)S(1)}, bf16[256,384]{1,0:T(8,128)(2,1)}, u32[]{:S(2)}) copy-start(bf16[256,384]{1,0:T(8,128)(2,1)} %param.7) | copy-start | bytes 589828
  11.6 22.2 %all-to-all-start.1 = ((bf16[16,32,384]{2,1,0:T(8,128)(2,1)}), bf16[16,32,384]{2,1,0:T(8,128)(2,1)S(1)}, u32[]{:S(2)}, u32[]{:S(2)}) async-start(bf16[16,32,384]{2,1,0:T(8,128)(2,1)} %pad_maximum_fusion), calls=%async_computation.1 | async-start | bytes 786432 | tf_op jit(solution)/shard_map/all_to_all | solution.py:101
  34.8 18.1 %all-to-all-start = ((bf16[4,256,384]{2,1,0:T(8,128)(2,1)}), bf16[4,256,384]{2,1,0:T(8,128)(2,1)S(1)}, u32[]{:S(2)}, u32[]{:S(2)}) async-start(bf16[4,256,384]{2,1,0:T(8,128)(2,1)} %stack.2), calls=%async_computation | async-start | bytes 1572864 | tf_op jit(solution)/shard_map/all_to_all | solution.py:73
  39.3 15.0 %copy-start.1 = (bf16[384,384]{1,0:T(8,128)(2,1)S(1)}, bf16[384,384]{1,0:T(8,128)(2,1)}, u32[]{:S(2)}) copy-start(bf16[384,384]{1,0:T(8,128)(2,1)} %param.8) | copy-start | bytes 884740
  39.3 43.3 %reduce-scatter.2.cloned.1.call-start = ((), (), s32[]{:S(2)}) async-start(), calls=%async_computation.3 | async-start | bytes 2621440 | tf_op jit(solution)/shard_map/reduce_scatter | solution.py:122
  56.5 78.0 %all-gather.3.cloned.1.call-start = ((), (), s32[]{:S(2)}) async-start(), calls=%async_computation.4 | async-start | bytes 1114112 | tf_op jit(solution)/shard_map/all_gather | solution.py:133
Sparse Core Ops, SparseCore 0:
  56.6 25.9 reduce-scatter.1
  85.6 48.8 all-gather.2
